TPU v7x, 512 devices: a whole 4x8x8 slice. The times are simulated.
512 devices in a mesh: dp: 8 (over y_hi, x), expert: 64 (over y_lo, z, core).
Axes of the slice: x: 4, y: 8 (y_hi: 2, y_lo: 4; y = y_hi * 4 + y_lo), z: 8, core: 2. Of those that a mesh axis runs over, the one named last changes fastest.
Arguments:
- tokens: bfloat16 [8192, 2560], P(('dp', 'expert')), may hold values from -6 to 6
- grad_out: bfloat16 [8192, 2560], P(('dp', 'expert')), may hold values from -6 to 6
- expert_ids: int32 [8192, 2], P(('dp', 'expert')), may hold values from 0 to 63, as said below
- gates: bfloat16 [8192, 2], P(('dp', 'expert')), may hold values from 0.099609375 to 1
- w_gate: bfloat16 [64, 2560, 1024], P('expert', None, 'dp'), may hold values from -0.125 to 0.125
- w_up: bfloat16 [64, 2560, 1024], P('expert', None, 'dp'), may hold values from -0.125 to 0.125
- w_down: bfloat16 [64, 1024, 2560], P('expert', 'dp'), may hold values from -0.1875 to 0.1875
Outputs:
- out_tokens: bfloat16 [8192, 2560], P(('dp', 'expert'))
- grad_tokens: bfloat16 [8192, 2560], P(('dp', 'expert'))
- grad_gate: bfloat16 [64, 2560, 1024], P('expert', None, 'dp')
- grad_up: bfloat16 [64, 2560, 1024], P('expert', None, 'dp')
- grad_down: bfloat16 [64, 1024, 2560], P('expert', 'dp')
Inputs may be any that keep to these rules, and one draw needn't show every extreme that they name: `expert_ids`: each token names 2 different experts. Over the tokens of all devices at one index of expert taken together, one expert, the same at every index, is named exactly 8 times; a second one, also the same at every index, exactly 5 times; every other expert at most 5 times.
All inputs are finite; a program needn't handle non-finite values.
Results may differ from a plain program's by a relative error of at most 0.019.
Values may be sent and summed in bfloat16 or wider, within the bound.
No kernel may reach another device: no remote copies, remote signals or barrier semaphores. Data moves between devices by JAX's collectives and lax.ppermute only.
A program may use at most 128 MiB of HBM per device.

v0:
```python
import jax
import jax.numpy as jnp
from jax import lax
from jax.sharding import PartitionSpec as P


def expert_rows(rows_in, cot_in, gate_weight, up_weight, down_weight):
    gate_pre = jnp.dot(rows_in, gate_weight, preferred_element_type=jnp.float32)
    up_pre = jnp.dot(rows_in, up_weight, preferred_element_type=jnp.float32)
    hidden = (jax.nn.silu(gate_pre) * up_pre).astype(jnp.bfloat16)
    partial_value = jnp.dot(hidden, down_weight, preferred_element_type=jnp.float32).astype(
        jnp.bfloat16
    )
    first_dim = (((0,), (0,)), ((), ()))
    last_dim = (((1,), (1,)), ((), ()))
    grad_down = lax.dot_general(hidden, cot_in, first_dim, preferred_element_type=jnp.float32)
    d_hidden = lax.dot_general(cot_in, down_weight, last_dim, preferred_element_type=jnp.float32)
    sig = jax.nn.sigmoid(gate_pre)
    d_gate = (d_hidden * up_pre * sig * (1.0 + gate_pre * (1.0 - sig))).astype(jnp.bfloat16)
    d_up = (d_hidden * gate_pre * sig).astype(jnp.bfloat16)
    grad_gate = lax.dot_general(rows_in, d_gate, first_dim, preferred_element_type=jnp.float32)
    grad_up = lax.dot_general(rows_in, d_up, first_dim, preferred_element_type=jnp.float32)
    back_term = lax.dot_general(d_gate, gate_weight, last_dim, preferred_element_type=jnp.float32)
    back_term = (
        back_term + lax.dot_general(d_up, up_weight, last_dim, preferred_element_type=jnp.float32)
    ).astype(jnp.bfloat16)
    return (partial_value, back_term, grad_gate, grad_up, grad_down)


def collect_slots(values, slot_index, weights):
    taken = jnp.take(values, slot_index.reshape(-1), axis=0, mode="fill", fill_value=0)
    taken = taken.reshape(slot_index.shape[0], slot_index.shape[1], values.shape[1]).astype(
        jnp.float32
    )
    if weights is None:
        return jnp.sum(taken, axis=1)
    return jnp.sum(weights.astype(jnp.float32)[:, :, None] * taken, axis=1)


def body(tokens, grad_out, expert_ids, gates, w_gate, w_up, w_down):
    dp_count = lax.axis_size("dp")
    experts = lax.axis_size("expert")
    local_rows = tokens.shape[0]
    width = tokens.shape[1]
    top_count = expert_ids.shape[1]
    group_rows = dp_count * local_rows
    assigned = group_rows * top_count
    mean_slots = assigned // experts
    cap_hot = 2 * mean_slots
    side = 128
    extra = jnp.concatenate(
        [
            expert_ids.astype(jnp.bfloat16),
            gates,
            jnp.zeros((local_rows, side - 2 * top_count), jnp.bfloat16),
        ],
        axis=1,
    )
    packed = jnp.concatenate([tokens, grad_out, extra], axis=1)
    group = lax.all_gather(packed, "dp", axis=0, tiled=True)
    group_tokens = group[:, :width]
    group_grads = group[:, width : 2 * width]
    group_ids = group[:, 2 * width : 2 * width + top_count].astype(jnp.int32)
    group_gates = group[:, 2 * width + top_count : 2 * width + 2 * top_count]
    flat_ids = group_ids.reshape(-1)
    expert_range = jnp.arange(experts, dtype=jnp.int32)
    member = (flat_ids[:, None] == expert_range[None, :]).astype(jnp.int32)
    before = jnp.sum((jnp.cumsum(member, axis=0) - member) * member, axis=1)
    slot_count = experts * cap_hot
    slot_of = (flat_ids * cap_hot + before).astype(jnp.int32)
    owner = jnp.full((slot_count,), assigned, jnp.int32)
    owner = owner.at[slot_of].set(jnp.arange(assigned, dtype=jnp.int32), mode="drop")
    filled = owner < assigned
    safe = jnp.where(filled, owner, 0)
    tok = safe // top_count
    gate_of = jnp.where(filled, group_gates.reshape(-1)[safe].astype(jnp.float32), 0.0)
    rows_taken = jnp.where(filled[:, None], group_tokens[tok], jnp.zeros((), jnp.bfloat16))
    cot_taken = (gate_of[:, None] * group_grads[tok].astype(jnp.float32)).astype(jnp.bfloat16)
    send = jnp.concatenate([rows_taken, cot_taken], axis=1)
    arrived = lax.all_to_all(
        send.reshape(experts, cap_hot, 2 * width), "expert", 0, 0, tiled=True
    ).reshape(slot_count, 2 * width)
    partial_value, back_term, grad_gate, grad_up, grad_down = expert_rows(
        arrived[:, :width], arrived[:, width:], w_gate[0], w_up[0], w_down[0]
    )
    ret = jnp.concatenate([partial_value, back_term], axis=1)
    returned = lax.all_to_all(
        ret.reshape(experts, cap_hot, 2 * width), "expert", 0, 0, tiled=True
    ).reshape(slot_count, 2 * width)
    slot_pairs = slot_of.reshape(group_rows, top_count)
    out_part = collect_slots(returned[:, :width], slot_pairs, group_gates)
    back_part = collect_slots(returned[:, width:], slot_pairs, None)
    both = jnp.concatenate([out_part, back_part], axis=1).astype(jnp.bfloat16)
    spread = lax.all_to_all(both.reshape(dp_count, local_rows, 2 * width), "dp", 0, 0, tiled=True)
    total = jnp.sum(spread.astype(jnp.float32), axis=0).astype(jnp.bfloat16)
    return (
        total[:, :width],
        total[:, width:],
        grad_gate.astype(jnp.bfloat16)[None],
        grad_up.astype(jnp.bfloat16)[None],
        grad_down.astype(jnp.bfloat16)[None],
    )


def solution(mesh):
    in_specs = (
        P(("dp", "expert"), None),
        P(("dp", "expert"), None),
        P(("dp", "expert"), None),
        P(("dp", "expert"), None),
        P("expert", None, "dp"),
        P("expert", None, "dp"),
        P("expert", "dp", None),
    )
    out_specs = (
        P(("dp", "expert"), None),
        P(("dp", "expert"), None),
        P("expert", None, "dp"),
        P("expert", None, "dp"),
        P("expert", "dp", None),
    )
    return jax.shard_map(body, mesh=mesh, in_specs=in_specs, out_specs=out_specs, check_vma=False)
```

profile of v0, /device:TPU:56, one launch (start us, length us, event | category | flops | bytes accessed | tf_op | source)
XLA Modules:
  0.0 495.1 jit_solution(2697792149016737092)
XLA Ops:
  8.8 1.7 concatenate.19
  10.5 70.9 %all-gather.2.cloned.1.call-done = bf16[128,5248]{1,0:T(8,128)(2,1)} async-done(((bf16[16,5248]{1,0:T(8,128)(2,1)}), bf16[128,5248]{1,0:T(8,128)(2,1)}) %all-gather.2.cloned.1.call-update) | async-done | bytes 1343504 | tf_op jit(solution)/shard_map/all_gather | solution.py:60
  81.4 1.0 slice_convert_fusion.1
  84.6 1.4 scatter_custom_fusion
  86.3 3.4 gather_fusion.1
  89.9 3.5 gather_fusion.2
  93.4 3.5 gather_fusion
  96.8 2.4 fusion
  100.4 144.5 %all_to_all.15 = bf16[64,8,5120]{2,1,0:T(8,128)(2,1)S(1)} all-to-all(bf16[64,8,5120]{2,1,0:T(8,128)(2,1)S(1)} %pad_maximum_fusion), channel_id=1, replica_groups=mesh['dp'=8,'expert'=64] {'expert'}, dimensions={0} | all-to-all | bytes 10485760 | tf_op jit(solution)/shard_map/all_to_all | solution.py:80
  244.9 0.8 fusion.5
  246.4 0.8 fusion.11
  247.3 0.9 multiply_convert_fusion.2
  248.2 0.8 convolution_convert_fusion
  249.0 0.8 fusion.17
  249.9 0.9 add_convert_fusion
  250.8 3.1 maximum_bitcast_fusion
  253.9 14.9 %all-to-all-start.1 = ((bf16[64,8,5120]{2,1,0:T(8,128)(2,1)}), bf16[64,8,5120]{2,1,0:T(8,128)(2,1)}, u32[]{:S(2)}, u32[]{:S(2)}) async-start(bf16[64,8,5120]{2,1,0:T(8,128)(2,1)} %maximum_bitcast_fusion), calls=%async_computation.1 | async-start | bytes 10485760 | tf_op jit(solution)/shard_map/all_to_all | solution.py:87
  268.8 146.7 %all-to-all-done.1 = bf16[64,8,5120]{2,1,0:T(8,128)(2,1)} async-done(((bf16[64,8,5120]{2,1,0:T(8,128)(2,1)}), bf16[64,8,5120]{2,1,0:T(8,128)(2,1)}, u32[]{:S(2)}, u32[]{:S(2)}) %all-to-all-start.1) | async-done | bytes 5242912 | tf_op jit(solution)/shard_map/all_to_all | solution.py:87
  415.6 4.4 fusion.28
  420.0 5.9 %gather_fusion.3 = bf16[256,2560]{1,0:T(8,128)(2,1)} fusion(bf16[512,2560]{1,0:T(8,128)(2,1)} %get-tuple-element.10, s32[1024]{0:T(1024)S(1)} %pad_clamp_fusion), kind=kCustom, calls=%fused_computation.clone | custom fusion | bytes 2622464 | tf_op jit(solution)/shard_map/jit(_take)/gather | solution.py:31
  425.9 2.5 gather_fusion.4
  428.4 3.9 select_convert_fusion
  432.3 3.2 reshape.110
  435.6 4.0 convert_element_type.86
  439.5 5.3 %reduce.1 = bf16[128,2560]{1,0:T(8,128)(2,1)} reduce(bf16[128,2,2560]{2,1,0:T(2,128)(2,1)} %convert_element_type.86, bf16[]{:T(256)} %constant.21.clone.1), dimensions={1}, to_apply=%region_5.7.clone | reduce | flops 327680 | bytes 1966082 | tf_op jit(solution)/shard_map/reduce_sum | solution.py:36
  444.9 3.7 multiply_reduce_fusion
  448.5 1.2 pad_maximum_fusion.1
  449.8 9.2 %all-to-all-start.2 = ((bf16[8,16,5120]{2,1,0:T(8,128)(2,1)}), bf16[8,16,5120]{2,1,0:T(8,128)(2,1)S(1)}, u32[]{:S(2)}, u32[]{:S(2)}) async-start(bf16[8,16,5120]{2,1,0:T(8,128)(2,1)} %pad_maximum_fusion.1), calls=%async_computation.2 | async-start | bytes 2621440 | tf_op jit(solution)/shard_map/all_to_all | solution.py:94
  458.9 3.3 fusion.3
  462.2 3.6 fusion.1
  465.8 1.7 fusion.2
  467.6 19.8 %all-to-all-done.2 = bf16[8,16,5120]{2,1,0:T(8,128)(2,1)S(1)} async-done(((bf16[8,16,5120]{2,1,0:T(8,128)(2,1)}), bf16[8,16,5120]{2,1,0:T(8,128)(2,1)S(1)}, u32[]{:S(2)}, u32[]{:S(2)}) %all-to-all-start.2) | async-done | bytes 1310752 | tf_op jit(solution)/shard_map/all_to_all | solution.py:94
  (62 shorter events, 7.0 us)
Async XLA Ops:
  7.2 240.1 %copy-start = (bf16[1,2560,128]{2,1,0:T(8,128)(2,1)S(1)}, bf16[1,2560,128]{2,1,0:T(8,128)(2,1)}, u32[]{:S(2)}) copy-start(bf16[1,2560,128]{2,1,0:T(8,128)(2,1)} %param.14) | copy-start | bytes 1966084
  7.2 74.2 %all-gather.2.cloned.1.call-start = ((), (), s32[]{:S(2)}) async-start(), calls=%async_computation.3 | async-start | bytes 1511424 | tf_op jit(solution)/shard_map/all_gather | solution.py:60
  81.4 8.4 %copy-start.5 = (bf16[128,5248]{1,0:T(8,128)(2,1)S(1)}, bf16[128,5248]{1,0:T(8,128)(2,1)}, u32[]{:S(2)}) copy-start(bf16[128,5248]{1,0:T(8,128)(2,1)} %all-gather.2.cloned.1.call-done) | copy-start | bytes 4030468
  96.8 2.5 copy-start.3
  100.4 144.5 %copy-start.7 = (bf16[1,128,2560]{2,1,0:T(8,128)(2,1)S(1)}, bf16[1,128,2560]{2,1,0:T(8,128)(2,1)}, u32[]{:S(2)}) copy-start(bf16[1,128,2560]{2,1,0:T(8,128)(2,1)} %param.15) | copy-start | bytes 1966084
  244.9 2.4 copy-start.2
  244.9 1.5 copy-start.6
  248.2 1.7 copy-start.10
  248.2 1.7 copy-start.8
  253.9 161.7 %all-to-all-start.1 = ((bf16[64,8,5120]{2,1,0:T(8,128)(2,1)}), bf16[64,8,5120]{2,1,0:T(8,128)(2,1)}, u32[]{:S(2)}, u32[]{:S(2)}) async-start(bf16[64,8,5120]{2,1,0:T(8,128)(2,1)} %maximum_bitcast_fusion), calls=%async_computation.1 | async-start | bytes 10485760 | tf_op jit(solution)/shard_map/all_to_all | solution.py:87
  444.9 3.7 copy-start.4
  449.8 12.4 %copy-start.11 = (bf16[512,128]{1,0:T(8,128)(2,1)S(1)}, bf16[512,128]{1,0:T(8,128)(2,1)}, u32[]{:S(2)}) copy-start(bf16[512,128]{1,0:T(8,128)(2,1)} %copy-done.10) | copy-start | bytes 393220
  449.8 37.6 %all-to-all-start.2 = ((bf16[8,16,5120]{2,1,0:T(8,128)(2,1)}), bf16[8,16,5120]{2,1,0:T(8,128)(2,1)S(1)}, u32[]{:S(2)}, u32[]{:S(2)}) async-start(bf16[8,16,5120]{2,1,0:T(8,128)(2,1)} %pad_maximum_fusion.1), calls=%async_computation.2 | async-start | bytes 2621440 | tf_op jit(solution)/shard_map/all_to_all | solution.py:94
  458.9 6.8 %slice-start = ((s8[5242880]{0:T(1024)(128)(4,1)}), s8[4194304]{0:T(1024)(128)(4,1)S(1)}, s32[]{:S(2)}) async-start(s8[5242880]{0:T(1024)(128)(4,1)} %bitcast.67), calls=%async_computation.4 | async-start | bytes 8388608
  462.2 3.6 slice-start.1
  462.2 3.6 copy-start.9
  465.8 22.5 %copy-start.1 = (bf16[1,2560,128]{2,1,0:T(8,128)(2,1)S(1)}, bf16[1,2560,128]{2,1,0:T(8,128)(2,1)}, u32[]{:S(2)}) copy-start(bf16[1,2560,128]{2,1,0:T(8,128)(2,1)} %param.14) | copy-start | bytes 1966084
Sparse Core Ops, SparseCore 0:
  11.8 69.6 all-gather.1
where the time goes:
time: 496 us; the launch traced here: 495 us
  waiting for transfers between devices  237 us (48%)
  blocking collectives  145 us (29%)
  local copies, waits for them, and re-layouts  36.8 us (7%)
  other arithmetic  24.2 us (5%)
  starting transfers between devices  24.1 us (5%)
  between operations  14.3 us (3%)
  matrix products  13.7 us (3%)
    all_to_all x1, waiting for transfers between devices, body(): lax.all_to_all(ret.reshape(experts, cap_hot, 2 * width), 'expert', 0, 0,...  147 us
    all_to_all x1, blocking collectives, body(): lax.all_to_all(send.reshape(experts, cap_hot, 2 * width), 'expert', 0, 0,...  145 us
    all_gather x1, waiting for transfers between devices, body(): group = lax.all_gather(packed, 'dp', axis=0, tiled=True)  70.9 us
    all_to_all x1, waiting for transfers between devices, body(): lax.all_to_all(both.reshape(dp_count, local_rows, 2 * width), 'dp', 0, 0,...  19.8 us
    all_to_all x1, starting transfers between devices, body(): lax.all_to_all(ret.reshape(experts, cap_hot, 2 * width), 'expert', 0, 0,...  14.9 us
  transfers between devices with their start and end apart: 3, of which 3 were waited for; matrix products, arithmetic and copies ran while one was open for 2% of the time, Pallas kernels for 0%

commit v1 on v0

--- a/solution.py
+++ b/solution.py
@@ -57,7 +57,9 @@
         axis=1,
     )
     packed = jnp.concatenate([tokens, grad_out, extra], axis=1)
-    group = lax.all_gather(packed, "dp", axis=0, tiled=True)
+    group = jnp.concatenate(
+        lax.all_to_all(jnp.stack([packed] * lax.axis_size("dp")), "dp", 0, 0), axis=0
+    )
     group_tokens = group[:, :width]
     group_grads = group[:, width : 2 * width]
     group_ids = group[:, 2 * width : 2 * width + top_count].astype(jnp.int32)

time: 496 us -> 450 us (0.907)
  waiting for transfers between devices: 237 us -> 167 us
  blocking collectives: 145 us -> 187 us
  between operations: 14.3 us -> 0.95 us
    all_gather x1 -> x0, waiting for transfers between devices: 70.9 us -> none  [body(): group = lax.all_gather(packed, 'dp', axis=0, tiled=True)]
    all_to_all x0 -> x1, blocking collectives: none -> 28 us  [body(): lax.all_to_all(jnp.stack([packed] * lax.axis_size('dp')), 'dp', 0, 0)]
    all_to_all x1, blocking collectives: 145 us -> 159 us  [body(): lax.all_to_all(send.reshape(experts, cap_hot, 2 * width), 'expert', 0, 0,...]
  transfers between devices with their start and end apart: 3 -> 2, of which waited for: 3 -> 2; matrix products, arithmetic and copies ran while one was open for 2% -> 2% of each run, Pallas kernels for 0% -> 0%
where the time goes in v1:
time: 450 us
  blocking collectives  187 us (42%)
  waiting for transfers between devices  167 us (37%)
  local copies, waits for them, and re-layouts  36.3 us (8%)
  starting transfers between devices  22.8 us (5%)
  other arithmetic  22.6 us (5%)
  matrix products  13.6 us (3%)
    all_to_all x1, blocking collectives, body(): lax.all_to_all(send.reshape(experts, cap_hot, 2 * width), 'expert', 0, 0,...  159 us
    all_to_all x1, waiting for transfers between devices, body(): lax.all_to_all(ret.reshape(experts, cap_hot, 2 * width), 'expert', 0, 0,...  147 us
    all_to_all x1, blocking collectives, body(): lax.all_to_all(jnp.stack([packed] * lax.axis_size('dp')), 'dp', 0, 0)  28 us
    all_to_all x1, waiting for transfers between devices, body(): lax.all_to_all(both.reshape(dp_count, local_rows, 2 * width), 'dp', 0, 0,...  19.8 us
    all_to_all x1, starting transfers between devices, body(): lax.all_to_all(ret.reshape(experts, cap_hot, 2 * width), 'expert', 0, 0,...  14.9 us
  transfers between devices with their start and end apart: 2, of which 2 were waited for; matrix products, arithmetic and copies ran while one was open for 2% of the time, Pallas kernels for 0%

profile of v1, /device:TPU:56, one launch (start us, length us, event | category | flops | bytes accessed | tf_op | source)
XLA Modules:
  0.0 449.5 jit_solution(5705340264516507835)
XLA Ops:
  2.2 1.0 concatenate.19
  3.4 28.0 %all_to_all.20 = bf16[8,16,5248]{2,1,0:T(8,128)(2,1)S(1)} all-to-all(bf16[8,16,5248]{2,1,0:T(8,128)(2,1)S(1)} %stack.2), channel_id=1, replica_groups=mesh['dp'=8,'expert'=64] {'dp'}, dimensions={0} | all-to-all | bytes 2686976 | tf_op jit(solution)/shard_map/all_to_all | solution.py:61
  33.0 1.4 scatter_custom_fusion
  34.7 3.4 gather_fusion.1
  38.1 3.5 gather_fusion.2
  41.6 3.5 gather_fusion
  45.1 2.4 fusion
  47.9 0.8 pad_maximum_fusion
  48.7 158.7 %all_to_all.21 = bf16[64,8,5120]{2,1,0:T(8,128)(2,1)S(1)} all-to-all(bf16[64,8,5120]{2,1,0:T(8,128)(2,1)S(1)} %pad_maximum_fusion), channel_id=1, replica_groups=mesh['dp'=8,'expert'=64] {'expert'}, dimensions={0} | all-to-all | bytes 10485760 | tf_op jit(solution)/shard_map/all_to_all | solution.py:82
  207.4 0.8 fusion.5
  208.9 0.8 fusion.11
  209.8 0.9 multiply_convert_fusion.2
  210.7 0.8 convolution_convert_fusion
  211.5 0.8 fusion.17
  212.4 0.9 add_convert_fusion
  213.3 3.1 maximum_bitcast_fusion
  216.4 14.9 %all-to-all-start.2 = ((bf16[64,8,5120]{2,1,0:T(8,128)(2,1)}), bf16[64,8,5120]{2,1,0:T(8,128)(2,1)}, u32[]{:S(2)}, u32[]{:S(2)}) async-start(bf16[64,8,5120]{2,1,0:T(8,128)(2,1)} %maximum_bitcast_fusion), calls=%async_computation.2 | async-start | bytes 10485760 | tf_op jit(solution)/shard_map/all_to_all | solution.py:89
  231.3 146.7 %all-to-all-done.2 = bf16[64,8,5120]{2,1,0:T(8,128)(2,1)} async-done(((bf16[64,8,5120]{2,1,0:T(8,128)(2,1)}), bf16[64,8,5120]{2,1,0:T(8,128)(2,1)}, u32[]{:S(2)}, u32[]{:S(2)}) %all-to-all-start.2) | async-done | bytes 5242912 | tf_op jit(solution)/shard_map/all_to_all | solution.py:89
  378.1 4.4 fusion.28
  382.4 6.0 %gather_fusion.3 = bf16[256,2560]{1,0:T(8,128)(2,1)} fusion(bf16[512,2560]{1,0:T(8,128)(2,1)} %get-tuple-element.10, s32[1024]{0:T(1024)S(1)} %pad_clamp_fusion), kind=kCustom, calls=%fused_computation.clone | custom fusion | bytes 2622464 | tf_op jit(solution)/shard_map/jit(_take)/gather | solution.py:31
  388.4 2.5 gather_fusion.4
  390.9 3.9 select_convert_fusion
  394.8 3.2 reshape.116
  398.1 4.0 convert_element_type.86
  402.0 5.3 %reduce.1 = bf16[128,2560]{1,0:T(8,128)(2,1)} reduce(bf16[128,2,2560]{2,1,0:T(2,128)(2,1)} %convert_element_type.86, bf16[]{:T(256)} %constant.21.clone.1), dimensions={1}, to_apply=%region_5.7.clone | reduce | flops 327680 | bytes 1966082 | tf_op jit(solution)/shard_map/reduce_sum | solution.py:36
  407.4 3.7 multiply_reduce_fusion
  411.1 1.2 pad_maximum_fusion.1
  412.3 7.9 %all-to-all-start.3 = ((bf16[8,16,5120]{2,1,0:T(8,128)(2,1)}), bf16[8,16,5120]{2,1,0:T(8,128)(2,1)S(1)}, u32[]{:S(2)}, u32[]{:S(2)}) async-start(bf16[8,16,5120]{2,1,0:T(8,128)(2,1)} %pad_maximum_fusion.1), calls=%async_computation.3 | async-start | bytes 2621440 | tf_op jit(solution)/shard_map/all_to_all | solution.py:96
  420.2 3.3 fusion.3
  423.5 3.6 fusion.1
  427.1 1.7 fusion.2
  428.8 19.8 %all-to-all-done.3 = bf16[8,16,5120]{2,1,0:T(8,128)(2,1)S(1)} async-done(((bf16[8,16,5120]{2,1,0:T(8,128)(2,1)}), bf16[8,16,5120]{2,1,0:T(8,128)(2,1)S(1)}, u32[]{:S(2)}, u32[]{:S(2)}) %all-to-all-start.3) | async-done | bytes 1310752 | tf_op jit(solution)/shard_map/all_to_all | solution.py:96
  (59 shorter events, 5.6 us)
Async XLA Ops:
  0.6 209.1 %copy-start = (bf16[1,2560,128]{2,1,0:T(8,128)(2,1)S(1)}, bf16[1,2560,128]{2,1,0:T(8,128)(2,1)}, u32[]{:S(2)}) copy-start(bf16[1,2560,128]{2,1,0:T(8,128)(2,1)} %param.14) | copy-start | bytes 1966084
  45.1 2.5 copy-start.3
  48.7 158.7 %copy-start.6 = (bf16[1,128,2560]{2,1,0:T(8,128)(2,1)S(1)}, bf16[1,128,2560]{2,1,0:T(8,128)(2,1)}, u32[]{:S(2)}) copy-start(bf16[1,128,2560]{2,1,0:T(8,128)(2,1)} %param.15) | copy-start | bytes 1966084
  207.4 2.4 copy-start.2
  207.4 1.5 copy-start.5
  210.7 1.7 copy-start.9
  210.7 1.7 copy-start.7
  216.4 161.7 %all-to-all-start.2 = ((bf16[64,8,5120]{2,1,0:T(8,128)(2,1)}), bf16[64,8,5120]{2,1,0:T(8,128)(2,1)}, u32[]{:S(2)}, u32[]{:S(2)}) async-start(bf16[64,8,5120]{2,1,0:T(8,128)(2,1)} %maximum_bitcast_fusion), calls=%async_computation.2 | async-start | bytes 10485760 | tf_op jit(solution)/shard_map/all_to_all | solution.py:89
  407.4 3.7 copy-start.4
  412.3 11.2 %copy-start.10 = (bf16[512,128]{1,0:T(8,128)(2,1)S(1)}, bf16[512,128]{1,0:T(8,128)(2,1)}, u32[]{:S(2)}) copy-start(bf16[512,128]{1,0:T(8,128)(2,1)} %copy-done.9) | copy-start | bytes 393220
  412.3 36.3 %all-to-all-start.3 = ((bf16[8,16,5120]{2,1,0:T(8,128)(2,1)}), bf16[8,16,5120]{2,1,0:T(8,128)(2,1)S(1)}, u32[]{:S(2)}, u32[]{:S(2)}) async-start(bf16[8,16,5120]{2,1,0:T(8,128)(2,1)} %pad_maximum_fusion.1), calls=%async_computation.3 | async-start | bytes 2621440 | tf_op jit(solution)/shard_map/all_to_all | solution.py:96
  420.2 6.8 %slice-start = ((s8[5242880]{0:T(1024)(128)(4,1)}), s8[4194304]{0:T(1024)(128)(4,1)S(1)}, s32[]{:S(2)}) async-start(s8[5242880]{0:T(1024)(128)(4,1)} %bitcast.68), calls=%async_computation.4 | async-start | bytes 8388608
  423.5 3.6 slice-start.1
  423.5 3.6 copy-start.8
  427.0 22.5 %copy-start.1 = (bf16[1,2560,128]{2,1,0:T(8,128)(2,1)S(1)}, bf16[1,2560,128]{2,1,0:T(8,128)(2,1)}, u32[]{:S(2)}) copy-start(bf16[1,2560,128]{2,1,0:T(8,128)(2,1)} %param.14) | copy-start | bytes 1966084
